TPU v7x, 256 devices: a whole 4x4x8 slice. The times are simulated.
256 devices in a mesh: dp: 8 (over y, core), seq: 32 (over x, z).
Axes of the slice: x: 4, y: 4, z: 8, core: 2. Of those that a mesh axis runs over, the one named last changes fastest.
Arguments:
- queries: bfloat16 [16, 2048, 1536], P('dp', 'seq'), may hold values from -6 to 6
- key_rows: bfloat16 [16, 2048, 1536], P('dp', 'seq'), may hold values from -6 to 6
- value_rows: bfloat16 [16, 2048, 1536], P('dp', 'seq'), may hold values from -6 to 6
- layer_input: bfloat16 [16, 2048, 1536], P('dp', 'seq'), may hold values from -6 to 6
- utt_lengths: int32 [16], P('dp'), may hold values from 512 to 2048, as said below
- out_weight: bfloat16 [1536, 1536], replicated, may hold values from -0.15625 to 0.15625
- conv_kernel: bfloat16 [31, 1536], replicated, may hold values from -1 to 1
- conv_cotangent: bfloat16 [16, 2048, 1536], P('dp', 'seq'), may hold values from -6 to 6
- pick_weight: int32 [23592], replicated, may hold values from 0 to 2359295
- pick_kernel: int32 [476], replicated, may hold values from 0 to 47615
Outputs:
- conv_out: bfloat16 [16, 2048, 1536], P('dp', 'seq')
- context_grad: bfloat16 [16, 2048, 1536], P('dp', 'seq')
- weight_picks: float32 [23592], replicated
- kernel_picks: float32 [476], replicated
Inputs may be any that keep to these rules, and one draw needn't show every extreme that they name: `utt_lengths`: the first utterance fills all 2048 slots and the last has 512 valid frames.
All inputs are finite; a program needn't handle non-finite values.
Results may differ from a plain program's by a relative error of at most 0.0056.
Values may be sent and summed in bfloat16 or wider, within the bound.
No kernel may reach another device: no remote copies, remote signals or barrier semaphores. Data moves between devices by JAX's collectives and lax.ppermute only.
A program may use at most 128 MiB of HBM per device.

v0:
```python
import math
import jax
import jax.numpy as jnp
from jax import lax
from jax.sharding import PartitionSpec as P

HEADS = 16
neg_big = -1e30


def padded(value, sides, width):
    for axis, dim in sides:
        count, length = (lax.axis_size(axis), value.shape[dim])
        up = [(i, (i + 1) % count) for i in range(count - 1)]
        down = [(j, i) for i, j in up]
        last = lax.slice_in_dim(value, length - width, length, axis=dim)
        leading = lax.slice_in_dim(value, 0, width, axis=dim)
        before = lax.ppermute(last, axis, up)
        after = lax.ppermute(leading, axis, down)
        value = jnp.concatenate([before, value, after], axis=dim)
    return value


def softmax_rows(scores, key_ok):
    scores = jnp.where(key_ok, scores, neg_big)
    row_max = jnp.max(scores, axis=-1, keepdims=True)
    probs = jnp.exp(scores - row_max)
    return (probs.astype(jnp.bfloat16), jnp.sum(probs, axis=-1))


def pick_entries(table, picks):
    flat = table.reshape(-1)
    lane = math.gcd(flat.shape[0], 128)
    blocks = flat.reshape(flat.shape[0] // lane, lane)
    chosen = jnp.take(blocks, picks // lane, axis=0)
    lane_ids = jnp.arange(lane, dtype=jnp.int32)
    hit = lane_ids[None, :] == (picks % lane)[:, None]
    return jnp.sum(jnp.where(hit, chosen, jnp.float32(0.0)), axis=1)


def on_device(
    queries,
    key_rows,
    value_rows,
    layer_input,
    utt_lengths,
    out_weight,
    conv_kernel,
    conv_cotangent,
    pick_weight,
    pick_kernel,
):
    local_utts, frames_dev, width = queries.shape
    seq_count = lax.axis_size("seq")
    full_frames = frames_dev * seq_count
    head_size = width // HEADS
    score_scale = 1.0 / math.sqrt(head_size)
    first_frame = lax.axis_index("seq") * frames_dev
    local_ids = first_frame + jnp.arange(frames_dev, dtype=jnp.int32)
    valid_rows = (local_ids[None, :] < utt_lengths[:, None]).astype(jnp.float32)
    all_keys, all_values = (
        lax.all_gather(key_rows, "seq", axis=1, tiled=True),
        lax.all_gather(value_rows, "seq", axis=1, tiled=True),
    )
    full_ids = jnp.arange(full_frames, dtype=jnp.int32)

    def one_utt(item):
        query_utt, key_utt, value_utt, length_utt = item
        query_heads = query_utt.reshape(frames_dev, HEADS, head_size)
        key_heads = key_utt.reshape(full_frames, HEADS, head_size)
        value_heads = value_utt.reshape(full_frames, HEADS, head_size)
        scores = (
            jnp.einsum("qhd,khd->hqk", query_heads, key_heads, preferred_element_type=jnp.float32)
            * score_scale
        )
        weights, denom = softmax_rows(scores, (full_ids < length_utt)[None, None, :])
        out_rows = jnp.einsum(
            "hqk,khd->qhd", weights, value_heads, preferred_element_type=jnp.float32
        )
        out_rows = out_rows / denom.transpose(1, 0)[:, :, None]
        return out_rows.astype(jnp.bfloat16).reshape(frames_dev, width)

    context = lax.map(one_utt, (queries, all_keys, all_values, utt_lengths))
    context_flat = context.reshape(local_utts * frames_dev, width)
    projected = jnp.dot(context_flat, out_weight, preferred_element_type=jnp.float32).reshape(
        local_utts, frames_dev, width
    )
    hidden = ((layer_input.astype(jnp.float32) + projected) * valid_rows[:, :, None]).astype(
        jnp.bfloat16
    )
    tap_count = conv_kernel.shape[0]
    half_taps = (tap_count - 1) // 2
    kernel_f = conv_kernel.astype(jnp.float32)
    hidden_pad = padded(hidden, (("seq", 1),), half_taps)
    cot_f = conv_cotangent.astype(jnp.float32)
    conv_sum = jnp.zeros((local_utts, frames_dev, width), jnp.float32)
    kernel_rows = []
    for offset in range(tap_count):
        window = hidden_pad[:, offset : offset + frames_dev].astype(jnp.float32)
        conv_sum = conv_sum + kernel_f[offset] * window
        kernel_rows.append(jnp.sum(window * cot_f, axis=(0, 1)))
    conv_out = conv_sum.astype(jnp.bfloat16)
    kernel_grad = jnp.stack(kernel_rows)
    cot_pad = padded(conv_cotangent, (("seq", 1),), half_taps).astype(jnp.float32)
    back_sum = jnp.zeros((local_utts, frames_dev, width), jnp.float32)
    for offset in range(tap_count):
        begin = 2 * half_taps - offset
        back_sum = back_sum + kernel_f[offset] * cot_pad[:, begin : begin + frames_dev]
    hidden_grad = (back_sum * valid_rows[:, :, None]).astype(jnp.bfloat16)
    grad_flat = hidden_grad.reshape(local_utts * frames_dev, width)
    weight_grad = lax.dot_general(
        context_flat, grad_flat, (((0,), (0,)), ((), ())), preferred_element_type=jnp.float32
    )
    context_grad = lax.dot_general(
        grad_flat, out_weight, (((1,), (1,)), ((), ())), preferred_element_type=jnp.float32
    )
    context_grad = context_grad.reshape(local_utts, frames_dev, width).astype(jnp.bfloat16)
    weight_vals = pick_entries(weight_grad, pick_weight)
    kernel_vals = pick_entries(kernel_grad, pick_kernel)
    weight_sum, kernel_sum = lax.psum((weight_vals, kernel_vals), ("dp", "seq"))
    total_slots = local_utts * lax.axis_size("dp") * full_frames
    norm_factor = 1.0 / math.sqrt(total_slots)
    return (conv_out, context_grad, weight_sum * norm_factor, kernel_sum * norm_factor)


def solution(mesh):
    placed = (
        P("dp", "seq", None),
        P("dp", "seq", None),
        P("dp", "seq", None),
        P("dp", "seq", None),
        P("dp"),
        P(),
        P(),
        P("dp", "seq", None),
        P(),
        P(),
    )
    return jax.shard_map(
        on_device,
        mesh=mesh,
        in_specs=placed,
        out_specs=(P("dp", "seq", None), P("dp", "seq", None), P(), P()),
        check_vma=False,
    )
```

profile of v0, /device:TPU:1, one launch (start us, length us, event | category | flops | bytes accessed | tf_op | source)
XLA Modules:
  0.0 756.6 jit_solution(8033392045944065864)
XLA Ops:
  7.2 2.1 copy.22
  9.4 2.2 copy.23
  12.6 4.4 collective-permute-start.2
  17.0 1.3 collective-permute-start.3
  23.4 1.6 compare_and_fusion
  25.0 1.6 add_select_fusion.1
  27.2 1.3 maximum_convert_fusion
  28.5 3.3 fusion.104
  32.1 2.4 fusion.34
  34.5 99.7 %all-gather.3.cloned.1.call-done = bf16[2,2048,1536]{2,0,1:T(2,128)(2,1)} async-done(((bf16[2,64,1536]{2,0,1:T(2,128)(2,1)}), bf16[2,2048,1536]{2,0,1:T(2,128)(2,1)}) %all-gather.3.cloned.1.call-update) | async-done | bytes 12582928 | tf_op jit(solution)/shard_map/all_gather | solution.py:63
  134.2 31.1 %copy.24 = bf16[2,2048,1536]{1,2,0:T(8,128)(2,1)} copy(bf16[2,2048,1536]{2,0,1:T(2,128)(2,1)} %all-gather.3.cloned.1.call-done) | data formatting | bytes 25165824
  165.4 88.2 %all-gather.5.cloned.1.call-done = bf16[2,2048,1536]{2,0,1:T(2,128)(2,1)} async-done(((bf16[2,64,1536]{2,0,1:T(2,128)(2,1)}), bf16[2,2048,1536]{2,0,1:T(2,128)(2,1)}) %all-gather.5.cloned.1.call-update) | async-done | bytes 12582928 | tf_op jit(solution)/shard_map/all_gather | solution.py:62
  253.6 31.1 %copy.25 = bf16[2,2048,1536]{1,2,0:T(8,128)(2,1)} copy(bf16[2,2048,1536]{2,0,1:T(2,128)(2,1)} %all-gather.5.cloned.1.call-done) | data formatting | bytes 25165824
  284.7 51.8 %while.11 = (s32[]{:T(128)}, bf16[2,64,1536]{2,1,0:T(8,128)(2,1)S(1)}, bf16[2,2048,1536]{1,2,0:T(8,128)(2,1)}, s32[2]{0:T(128)S(1)}, bf16[2,64,1536]{2,1,0:T(8,1...) while((s32[]{:T(128)}, bf16[2,64,1536]{2,1,0:T(8,128)(2,1)S(1)}, ...), condition=%wide.region_3.4_spmd.clone, body=%wide.region_0.3_spmd.clone.sunk | while | flops 828571648 | bytes 65302632 | solution.py:83
  284.7 11.9 %constant_dynamic-slice_fusion.5 = (bf16[1,2048,1536]{1,2,0:T(8,128)(2,1)}, bf16[1,2048,1536]{1,2,0:T(8,128)(2,1)}) fusion(bf16[2,2048,1536]{1,2,0:T(8,128)(2,1)} %get-tuple-element.212, s32[]{:T(128)} %get-tuple-element.200, bf16[2,2048,1536]{1,2,0:T(8,128)(2,1)} %get-tuple-element.209), kind=kLoop, calls=%fused_computation.20.clone.1 | loop fusion | bytes 25165828 | tf_op jit(solution)/shard_map/while/body/jit(dynamic_index_in_dim)/dynamic_slice | solution.py:83
  298.2 5.0 fusion.182
  303.2 1.9 fusion.183
  305.1 5.1 fusion.184
  310.6 11.9 %constant_dynamic-slice_fusion.5 = (bf16[1,2048,1536]{1,2,0:T(8,128)(2,1)}, bf16[1,2048,1536]{1,2,0:T(8,128)(2,1)}) fusion(bf16[2,2048,1536]{1,2,0:T(8,128)(2,1)} %get-tuple-element.212, s32[]{:T(128)} %get-tuple-element.200, bf16[2,2048,1536]{1,2,0:T(8,128)(2,1)} %get-tuple-element.209), kind=kLoop, calls=%fused_computation.20.clone.1 | loop fusion | bytes 25165828 | tf_op jit(solution)/shard_map/while/body/jit(dynamic_index_in_dim)/dynamic_slice | solution.py:83
  324.1 5.0 fusion.182
  329.1 1.9 fusion.183
  331.0 5.1 fusion.184
  336.6 5.0 convolution_bitcast_fusion
  342.4 10.5 %reshape_reshape.6 = f32[18432,128]{1,0:T(8,128)} reshape(f32[1536,1536]{1,0:T(8,128)} %convolution_bitcast_fusion) | data formatting | bytes 18874368 | tf_op jit(solution)/shard_map/reshape;reshape | solution.py:34
  353.0 48.0 %gather_fusion = f32[23592,128]{1,0:T(8,128)} fusion(f32[18432,128]{1,0:T(8,128)} %reshape_reshape.6, s32[24576]{0:T(1024)S(1)} %pad_clamp_fusion), kind=kCustom, calls=%fused_computation | custom fusion | bytes 24252576 | tf_op jit(solution)/shard_map/jit(_take)/gather | solution.py:35
  401.3 22.9 %select_reduce_fusion = f32[23592]{0:T(1024)} fusion(f32[23592,128]{1,0:T(8,128)} %gather_fusion, s32[23592]{0:T(1024)S(1)} %copy-done.2, pred[23592]{0:T(1024)(128)(4,1)S(1)} %copy-done.4), kind=kLoop, calls=%fused_computation.25 | loop fusion | flops 12055512 | bytes 12291432 | tf_op jit(solution)/shard_map/reduce_sum | solution.py:38
  424.3 1.4 collective-permute-start
  427.0 235.6 %all-reduce.2.cloned.1.call-done = f32[23592]{0:T(1024)} async-done(((f32[23592]{0:T(1024)}), f32[23592]{0:T(1024)}) %all-reduce.2.cloned.1.call-update) | async-done | bytes 94384 | tf_op jit(solution)/shard_map/psum | solution.py:120
  662.5 1.5 broadcast_multiply_fusion
  665.4 1.3 fusion.101
  670.6 74.1 %psum.15 = f32[476]{0:T(512)S(1)} all-reduce(f32[476]{0:T(512)S(1)} %select_reduce_fusion.1), channel_id=1, replica_groups=mesh['dp'=8,'seq'=32] {'dp','seq'}, use_global_device_ids=true, to_apply=%region_38.39 | all-reduce | flops 476 | bytes 3808 | tf_op jit(solution)/shard_map/psum | solution.py:120
  745.6 4.5 fusion.70
  (229 shorter events, 18.2 us)
Async XLA Ops:
  7.2 127.1 %all-gather.3.cloned.1.call-start = ((), (), s32[]{:S(2)}) async-start(), calls=%async_computation | async-start | bytes 12976128 | tf_op jit(solution)/shard_map/all_gather | solution.py:63
  9.4 244.2 %all-gather.5.cloned.1.call-start = ((), (), s32[]{:S(2)}) async-start(), calls=%async_computation.1 | async-start | bytes 12976128 | tf_op jit(solution)/shard_map/all_gather | solution.py:62
  11.6 650.9 %all-reduce.2.cloned.1.call-start = ((), (), s32[]{:S(2)}) async-start(), calls=%async_computation.2 | async-start | bytes 196608 | tf_op jit(solution)/shard_map/psum | solution.py:120
  12.6 14.5 %collective-permute-start.2 = (bf16[2,15,1536]{2,1,0:T(8,128)(2,1)S(1)}, bf16[2,15,1536]{2,1,0:T(8,128)(2,1)S(1)}, u32[]{:S(2)}, u32[]{:S(2)}) collective-permute-start(bf16[2,15,1536]{2,1,0:T(8,128)(2,1)S(1)} %get-tuple-element.144), channel_id=1, source_target_pairs={{0,1},{1,2},{2,3},{3,4},{4,5},{5,6},{6,7},{7,8},{8,9},{9,10},{10,1... | collective-permute-start | bytes 276488 | tf_op jit(solution)/shard_map/ppermute | solution.py:18
  17.0 10.1 %collective-permute-start.3 = (bf16[2,15,1536]{2,1,0:T(8,128)(2,1)S(1)}, bf16[2,15,1536]{2,1,0:T(8,128)(2,1)S(1)}, u32[]{:S(2)}, u32[]{:S(2)}) collective-permute-start(bf16[2,15,1536]{2,1,0:T(8,128)(2,1)S(1)} %get-tuple-element.145), channel_id=1, source_target_pairs={{1,0},{2,1},{3,2},{4,3},{5,4},{6,5},{7,6},{8,7},{9,8},{10,9},{11,1... | collective-permute-start | bytes 276488 | tf_op jit(solution)/shard_map/ppermute | solution.py:19
  401.0 344.3 %copy-start.6 = (f32[1536]{0:T(1024)S(1)}, f32[1536]{0:T(1024)}, u32[]{:S(2)}) copy-start(f32[1536]{0:T(1024)} %copy-done.5) | copy-start | bytes 18436
  401.0 344.3 %copy-start.8 = (f32[1536]{0:T(1024)S(1)}, f32[1536]{0:T(1024)}, u32[]{:S(2)}) copy-start(f32[1536]{0:T(1024)} %copy-done.7) | copy-start | bytes 18436
  401.0 344.3 %copy-start.10 = (f32[1536]{0:T(1024)S(1)}, f32[1536]{0:T(1024)}, u32[]{:S(2)}) copy-start(f32[1536]{0:T(1024)} %copy-done.9) | copy-start | bytes 18436
  401.0 344.3 %copy-start.12 = (f32[1536]{0:T(1024)S(1)}, f32[1536]{0:T(1024)}, u32[]{:S(2)}) copy-start(f32[1536]{0:T(1024)} %copy-done.11) | copy-start | bytes 18436
  401.0 344.3 %copy-start.14 = (f32[1536]{0:T(1024)S(1)}, f32[1536]{0:T(1024)}, u32[]{:S(2)}) copy-start(f32[1536]{0:T(1024)} %copy-done.13) | copy-start | bytes 18436
  401.0 344.3 %copy-start.16 = (f32[1536]{0:T(1024)S(1)}, f32[1536]{0:T(1024)}, u32[]{:S(2)}) copy-start(f32[1536]{0:T(1024)} %copy-done.15) | copy-start | bytes 18436
  401.0 344.3 %copy-start.18 = (f32[1536]{0:T(1024)S(1)}, f32[1536]{0:T(1024)}, u32[]{:S(2)}) copy-start(f32[1536]{0:T(1024)} %copy-done.17) | copy-start | bytes 18436
  401.0 344.3 %copy-start.20 = (f32[1536]{0:T(1024)S(1)}, f32[1536]{0:T(1024)}, u32[]{:S(2)}) copy-start(f32[1536]{0:T(1024)} %copy-done.19) | copy-start | bytes 18436
  401.1 344.3 %copy-start.22 = (f32[1536]{0:T(1024)S(1)}, f32[1536]{0:T(1024)}, u32[]{:S(2)}) copy-start(f32[1536]{0:T(1024)} %copy-done.21) | copy-start | bytes 18436
  401.1 344.3 %copy-start.24 = (f32[1536]{0:T(1024)S(1)}, f32[1536]{0:T(1024)}, u32[]{:S(2)}) copy-start(f32[1536]{0:T(1024)} %copy-done.23) | copy-start | bytes 18436
  401.1 344.3 %copy-start.26 = (f32[1536]{0:T(1024)S(1)}, f32[1536]{0:T(1024)}, u32[]{:S(2)}) copy-start(f32[1536]{0:T(1024)} %copy-done.25) | copy-start | bytes 18436
  401.1 344.3 %copy-start.28 = (f32[1536]{0:T(1024)S(1)}, f32[1536]{0:T(1024)}, u32[]{:S(2)}) copy-start(f32[1536]{0:T(1024)} %copy-done.27) | copy-start | bytes 18436
  401.1 344.3 %copy-start.30 = (f32[1536]{0:T(1024)S(1)}, f32[1536]{0:T(1024)}, u32[]{:S(2)}) copy-start(f32[1536]{0:T(1024)} %copy-done.29) | copy-start | bytes 18436
  401.1 344.3 %copy-start.32 = (f32[1536]{0:T(1024)S(1)}, f32[1536]{0:T(1024)}, u32[]{:S(2)}) copy-start(f32[1536]{0:T(1024)} %copy-done.31) | copy-start | bytes 18436
  401.1 344.3 %copy-start.34 = (f32[1536]{0:T(1024)S(1)}, f32[1536]{0:T(1024)}, u32[]{:S(2)}) copy-start(f32[1536]{0:T(1024)} %copy-done.33) | copy-start | bytes 18436
  401.1 344.3 %copy-start.36 = (f32[1536]{0:T(1024)S(1)}, f32[1536]{0:T(1024)}, u32[]{:S(2)}) copy-start(f32[1536]{0:T(1024)} %copy-done.35) | copy-start | bytes 18436
  401.1 344.3 %copy-start.38 = (f32[1536]{0:T(1024)S(1)}, f32[1536]{0:T(1024)}, u32[]{:S(2)}) copy-start(f32[1536]{0:T(1024)} %copy-done.37) | copy-start | bytes 18436
  401.1 344.3 %copy-start.40 = (f32[1536]{0:T(1024)S(1)}, f32[1536]{0:T(1024)}, u32[]{:S(2)}) copy-start(f32[1536]{0:T(1024)} %copy-done.39) | copy-start | bytes 18436
  401.2 344.3 %copy-start.42 = (f32[1536]{0:T(1024)S(1)}, f32[1536]{0:T(1024)}, u32[]{:S(2)}) copy-start(f32[1536]{0:T(1024)} %copy-done.41) | copy-start | bytes 18436
  401.2 344.3 %copy-start.44 = (f32[1536]{0:T(1024)S(1)}, f32[1536]{0:T(1024)}, u32[]{:S(2)}) copy-start(f32[1536]{0:T(1024)} %copy-done.43) | copy-start | bytes 18436
  401.2 344.3 %copy-start.46 = (f32[1536]{0:T(1024)S(1)}, f32[1536]{0:T(1024)}, u32[]{:S(2)}) copy-start(f32[1536]{0:T(1024)} %copy-done.45) | copy-start | bytes 18436
  401.2 344.3 %copy-start.48 = (f32[1536]{0:T(1024)S(1)}, f32[1536]{0:T(1024)}, u32[]{:S(2)}) copy-start(f32[1536]{0:T(1024)} %copy-done.47) | copy-start | bytes 18436
  401.2 344.3 %copy-start.50 = (f32[1536]{0:T(1024)S(1)}, f32[1536]{0:T(1024)}, u32[]{:S(2)}) copy-start(f32[1536]{0:T(1024)} %copy-done.49) | copy-start | bytes 18436
  401.2 344.3 %copy-start.52 = (f32[1536]{0:T(1024)S(1)}, f32[1536]{0:T(1024)}, u32[]{:S(2)}) copy-start(f32[1536]{0:T(1024)} %copy-done.51) | copy-start | bytes 18436
  401.2 344.3 %copy-start.54 = (f32[1536]{0:T(1024)S(1)}, f32[1536]{0:T(1024)}, u32[]{:S(2)}) copy-start(f32[1536]{0:T(1024)} %copy-done.53) | copy-start | bytes 18436
  424.3 239.8 %collective-permute-start = (bf16[2,15,1536]{2,1,0:T(8,128)(2,1)S(1)}, bf16[2,15,1536]{2,1,0:T(8,128)(2,1)S(1)}, u32[]{:S(2)}, u32[]{:S(2)}) collective-permute-start(bf16[2,15,1536]{2,1,0:T(8,128)(2,1)S(1)} %get-tuple-element.146), channel_id=1, source_target_pairs={{0,1},{1,2},{2,3},{3,4},{4,5},{5,6},{6,7},{7,8},{8,9},{9,10},{10,1... | collective-permute-start | bytes 276488 | tf_op jit(solution)/shard_map/ppermute | solution.py:18
  425.7 239.7 %collective-permute-start.1 = (bf16[2,15,1536]{2,1,0:T(8,128)(2,1)S(1)}, bf16[2,15,1536]{2,1,0:T(8,128)(2,1)S(1)}, u32[]{:S(2)}, u32[]{:S(2)}) collective-permute-start(bf16[2,15,1536]{2,1,0:T(8,128)(2,1)S(1)} %get-tuple-element.147), channel_id=1, source_target_pairs={{1,0},{2,1},{3,2},{4,3},{5,4},{6,5},{7,6},{8,7},{9,8},{10,9},{11,1... | collective-permute-start | bytes 276488 | tf_op jit(solution)/shard_map/ppermute | solution.py:19
  (50 other events, 3870.6 us)
Sparse Core Ops, SparseCore 0:
  11.2 123.0 all-gather.2
  136.8 116.7 all-gather.4
  424.3 238.1 all-reduce.1
where the time goes:
time: 759 us; the launch traced here: 757 us
  waiting for transfers between devices  424 us (56%)
  local copies, waits for them, and re-layouts  155 us (20%)
  blocking collectives  74.1 us (10%)
  other arithmetic  51.7 us (7%)
  matrix products  28.4 us (4%)
  between operations  15.2 us (2%)
  starting transfers between devices  8.5 us (1%)
    psum x1, waiting for transfers between devices, on_device(): weight_sum, kernel_sum = lax.psum((weight_vals, kernel_vals), ('dp', 'seq'))  236 us
    all_gather x1, waiting for transfers between devices, on_device(): lax.all_gather(value_rows, 'seq', axis=1, tiled=True)  99.7 us
    all_gather x1, waiting for transfers between devices, on_device(): lax.all_gather(key_rows, 'seq', axis=1, tiled=True)  88.2 us
    psum x1, blocking collectives, on_device(): weight_sum, kernel_sum = lax.psum((weight_vals, kernel_vals), ('dp', 'seq'))  74.1 us
    unnamed x154, local copies, waits for them, and re-layouts  66.9 us
    gather x2, local copies, waits for them, and re-layouts, pick_entries(): chosen = jnp.take(blocks, picks // lane, axis=0)  49.1 us
    dynamic_slice x6, local copies, waits for them, and re-layouts, on_device(): context = lax.map(one_utt, (queries, all_keys, all_values, utt_lengths))  25.1 us
    reduce_sum x2, other arithmetic, pick_entries(): return jnp.sum(jnp.where(hit, chosen, jnp.float32(0.0)), axis=1)  23.2 us
  transfers between devices with their start and end apart: 7, of which 3 were waited for; matrix products, arithmetic and copies ran while one was open for 7% of the time, Pallas kernels for 0%

commit v1 on v0

--- a/solution.py
+++ b/solution.py
@@ -6,6 +6,13 @@
 
 HEADS = 16
 neg_big = -1e30
+
+
+def exchange_gather(x, axis, along):
+    peers = lax.axis_size(axis)
+    blocks = jnp.stack([x for _ in range(peers)])
+    blocks = lax.all_to_all(blocks, axis, split_axis=0, concat_axis=0)
+    return jnp.concatenate(blocks, axis=along)
 
 
 def padded(value, sides, width):
@@ -59,7 +66,7 @@
     local_ids = first_frame + jnp.arange(frames_dev, dtype=jnp.int32)
     valid_rows = (local_ids[None, :] < utt_lengths[:, None]).astype(jnp.float32)
     all_keys, all_values = (
-        lax.all_gather(key_rows, "seq", axis=1, tiled=True),
+        exchange_gather(key_rows, "seq", 1),
         lax.all_gather(value_rows, "seq", axis=1, tiled=True),
     )
     full_ids = jnp.arange(full_frames, dtype=jnp.int32)

time: 759 us -> 926 us (1.22)
  waiting for transfers between devices: 424 us -> 581 us
  starting transfers between devices: 8.5 us -> 22.3 us
    ppermute x2, waiting for transfers between devices: 0.01 us -> 344 us  [padded(): before = lax.ppermute(last, axis, up)]
    all_gather x1, waiting for transfers between devices: 99.7 us -> 0.01 us  [on_device(): lax.all_gather(value_rows, 'seq', axis=1, tiled=True)]
    all_gather x1 -> x0, waiting for transfers between devices: 88.2 us -> none  [on_device(): lax.all_gather(key_rows, 'seq', axis=1, tiled=True)]
    unnamed x154 -> x168, local copies, waits for them, and re-layouts: 66.9 us -> 32.7 us
    dynamic_slice x6 -> x10, local copies, waits for them, and re-layouts: 25.1 us -> 43.4 us  [on_device(): context = lax.map(one_utt, (queries, all_keys, all_values, utt_lengths))]
    all_to_all x0 -> x1, starting transfers between devices: none -> 12.1 us  [exchange_gather(): blocks = lax.all_to_all(blocks, axis, split_axis=0, concat_axis=0)]
    all_to_all x0 -> x1, local copies, waits for them, and re-layouts: none -> 10.9 us  [exchange_gather(): blocks = lax.all_to_all(blocks, axis, split_axis=0, concat_axis=0)]
  transfers between devices with their start and end apart: 7 -> 7, of which waited for: 3 -> 2; matrix products, arithmetic and copies ran while one was open for 7% -> 3% of each run, Pallas kernels for 0% -> 0%
where the time goes in v1:
time: 926 us; the launch traced here: 924 us
  waiting for transfers between devices  581 us (63%)
  local copies, waits for them, and re-layouts  156 us (17%)
  blocking collectives  74.1 us (8%)
  other arithmetic  46.4 us (5%)
  matrix products  28.4 us (3%)
  starting transfers between devices  22.3 us (2%)
  between operations  15.6 us (2%)
    ppermute x2, waiting for transfers between devices, padded(): before = lax.ppermute(last, axis, up)  344 us
    psum x1, waiting for transfers between devices, on_device(): weight_sum, kernel_sum = lax.psum((weight_vals, kernel_vals), ('dp', 'seq'))  237 us
    psum x1, blocking collectives, on_device(): weight_sum, kernel_sum = lax.psum((weight_vals, kernel_vals), ('dp', 'seq'))  74.1 us
    gather x2, local copies, waits for them, and re-layouts, pick_entries(): chosen = jnp.take(blocks, picks // lane, axis=0)  49.1 us
    dynamic_slice x10, local copies, waits for them, and re-layouts, on_device(): context = lax.map(one_utt, (queries, all_keys, all_values, utt_lengths))  43.4 us
    unnamed x168, local copies, waits for them, and re-layouts  32.7 us
    reduce_sum x2, other arithmetic, pick_entries(): return jnp.sum(jnp.where(hit, chosen, jnp.float32(0.0)), axis=1)  23.2 us
  transfers between devices with their start and end apart: 7, of which 2 were waited for; matrix products, arithmetic and copies ran while one was open for 3% of the time, Pallas kernels for 0%

profile of v1, /device:TPU:1, one launch (start us, length us, event | category | flops | bytes accessed | tf_op | source)
XLA Modules:
  0.0 923.9 jit_solution(9519200711261834282)
XLA Ops:
  7.2 7.1 stack.131
  14.3 12.1 %all-to-all-start = ((bf16[32,2,64,1536]{3,2,1,0:T(8,128)(2,1)}), bf16[32,2,64,1536]{3,2,1,0:T(8,128)(2,1)}, u32[]{:S(2)}, u32[]{:S(2)}) async-start(bf16[32,2,64,1536]{3,2,1,0:T(8,128)(2,1)} %stack.131), calls=%async_computation | async-start | bytes 25165824 | tf_op jit(solution)/shard_map/all_to_all | solution.py:14
  27.8 3.1 collective-permute-start.2
  30.8 1.3 collective-permute-start.3
  36.9 343.8 %collective-permute-done.2 = bf16[2,15,1536]{2,1,0:T(8,128)(2,1)S(1)} collective-permute-done((bf16[2,15,1536]{2,1,0:T(8,128)(2,1)S(1)}, bf16[2,15,1536]{2,1,0:T(8,128)(2,1)S(1)}, u32[]{:S(2)}, u32[]{:S(2)}) %collective-permute-start.2) | collective-permute-done | bytes 92192 | tf_op jit(solution)/shard_map/ppermute | solution.py:25
  380.9 3.3 fusion.104
  384.5 2.4 fusion.34
  386.9 10.9 %copy.23 = bf16[32,2,64,1536]{3,2,0,1:T(8,128)(2,1)} copy(bf16[32,2,64,1536]{3,2,1,0:T(8,128)(2,1)} %all-to-all-done) | data formatting | bytes 25165824 | tf_op jit(solution)/shard_map/all_to_all | solution.py:14
  397.8 31.2 %copy.24 = bf16[2,2048,1536]{1,2,0:T(8,128)(2,1)} copy(bf16[2,2048,1536]{2,0,1:T(2,128)(2,1)} %all-gather.2.cloned.1.call-done) | data formatting | bytes 25165824
  429.0 70.1 %while.11 = (s32[]{:T(128)}, bf16[2,64,1536]{2,1,0:T(8,128)(2,1)S(1)}, bf16[2,2048,1536]{1,2,0:T(8,128)(2,1)}, s32[2]{0:T(128)S(1)}, bf16[2,64,1536]{2,1,0:T(8,1...) while((s32[]{:T(128)}, bf16[2,64,1536]{2,1,0:T(8,128)(2,1)S(1)}, ...), condition=%wide.region_3.4_spmd.clone, body=%wide.region_0.3_spmd.clone.sunk | while | flops 828571648 | bytes 77885552 | solution.py:90
  430.3 5.9 constant_dynamic-slice_fusion.7
  436.1 8.7 copy.35
  445.0 5.0 fusion.182
  450.1 1.9 fusion.183
  452.0 6.6 constant_dynamic-slice_fusion.6
  458.5 5.1 fusion.184
  465.3 5.9 constant_dynamic-slice_fusion.7
  471.2 8.7 copy.35
  480.1 5.0 fusion.182
  485.1 1.9 fusion.183
  487.0 6.6 constant_dynamic-slice_fusion.6
  493.6 5.1 fusion.184
  499.2 5.0 convolution_bitcast_fusion
  505.1 10.6 %reshape_reshape.6 = f32[18432,128]{1,0:T(8,128)} reshape(f32[1536,1536]{1,0:T(8,128)} %convolution_bitcast_fusion) | data formatting | bytes 18874368 | tf_op jit(solution)/shard_map/reshape;reshape | solution.py:41
  515.6 48.0 %gather_fusion = f32[23592,128]{1,0:T(8,128)} fusion(f32[18432,128]{1,0:T(8,128)} %reshape_reshape.6, s32[24576]{0:T(1024)S(1)} %copy-done.4), kind=kCustom, calls=%fused_computation | custom fusion | bytes 24252576 | tf_op jit(solution)/shard_map/jit(_take)/gather | solution.py:42
  563.9 22.9 %select_reduce_fusion = f32[23592]{0:T(1024)} fusion(f32[23592,128]{1,0:T(8,128)} %gather_fusion, s32[23592]{0:T(1024)S(1)} %copy-done.3, pred[23592]{0:T(1024)(128)(4,1)S(1)} %copy-done.8), kind=kLoop, calls=%fused_computation.25 | loop fusion | flops 12055512 | bytes 12291432 | tf_op jit(solution)/shard_map/reduce_sum | solution.py:45
  588.2 4.4 collective-permute-start
  592.6 236.9 %all-reduce.2.cloned.1.call-done = f32[23592]{0:T(1024)} async-done(((f32[23592]{0:T(1024)}), f32[23592]{0:T(1024)}) %all-reduce.2.cloned.1.call-update) | async-done | bytes 94384 | tf_op jit(solution)/shard_map/psum | solution.py:127
  829.5 1.5 broadcast_multiply_fusion
  831.1 1.3 fusion.101
  837.6 74.1 %psum.15 = f32[476]{0:T(512)S(1)} all-reduce(f32[476]{0:T(512)S(1)} %select_reduce_fusion.1), channel_id=1, replica_groups=mesh['dp'=8,'seq'=32] {'dp','seq'}, use_global_device_ids=true, to_apply=%region_38.39 | all-reduce | flops 476 | bytes 3808 | tf_op jit(solution)/shard_map/psum | solution.py:127
  912.6 4.5 fusion.70
  (248 shorter events, 17.6 us)
Async XLA Ops:
  14.3 372.6 %all-to-all-start = ((bf16[32,2,64,1536]{3,2,1,0:T(8,128)(2,1)}), bf16[32,2,64,1536]{3,2,1,0:T(8,128)(2,1)}, u32[]{:S(2)}, u32[]{:S(2)}) async-start(bf16[32,2,64,1536]{3,2,1,0:T(8,128)(2,1)} %stack.131), calls=%async_computation | async-start | bytes 25165824 | tf_op jit(solution)/shard_map/all_to_all | solution.py:14
  26.4 371.4 %all-gather.2.cloned.1.call-start = ((), (), s32[]{:S(2)}) async-start(), calls=%async_computation.1 | async-start | bytes 12976128 | tf_op jit(solution)/shard_map/all_gather | solution.py:70
  27.7 801.9 %all-reduce.2.cloned.1.call-start = ((), (), s32[]{:S(2)}) async-start(), calls=%async_computation.2 | async-start | bytes 196608 | tf_op jit(solution)/shard_map/psum | solution.py:127
  27.8 352.9 %collective-permute-start.2 = (bf16[2,15,1536]{2,1,0:T(8,128)(2,1)S(1)}, bf16[2,15,1536]{2,1,0:T(8,128)(2,1)S(1)}, u32[]{:S(2)}, u32[]{:S(2)}) collective-permute-start(bf16[2,15,1536]{2,1,0:T(8,128)(2,1)S(1)} %get-tuple-element.148), channel_id=1, source_target_pairs={{0,1},{1,2},{2,3},{3,4},{4,5},{5,6},{6,7},{7,8},{8,9},{9,10},{10,1... | collective-permute-start | bytes 276488 | tf_op jit(solution)/shard_map/ppermute | solution.py:25
  30.8 349.9 %collective-permute-start.3 = (bf16[2,15,1536]{2,1,0:T(8,128)(2,1)S(1)}, bf16[2,15,1536]{2,1,0:T(8,128)(2,1)S(1)}, u32[]{:S(2)}, u32[]{:S(2)}) collective-permute-start(bf16[2,15,1536]{2,1,0:T(8,128)(2,1)S(1)} %get-tuple-element.149), channel_id=1, source_target_pairs={{1,0},{2,1},{3,2},{4,3},{5,4},{6,5},{7,6},{8,7},{9,8},{10,9},{11,1... | collective-permute-start | bytes 276488 | tf_op jit(solution)/shard_map/ppermute | solution.py:26
  32.4 351.8 %copy-start.48 = (f32[1536]{0:T(1024)}, f32[1536]{0:T(1024)S(1)}, u32[]{:S(2)}) copy-start(f32[1536]{0:T(1024)S(1)} %get-tuple-element.118) | copy-start | bytes 18436
  32.4 351.8 %copy-start.50 = (f32[1536]{0:T(1024)}, f32[1536]{0:T(1024)S(1)}, u32[]{:S(2)}) copy-start(f32[1536]{0:T(1024)S(1)} %get-tuple-element.119) | copy-start | bytes 18436
  32.4 351.8 %copy-start.52 = (f32[1536]{0:T(1024)}, f32[1536]{0:T(1024)S(1)}, u32[]{:S(2)}) copy-start(f32[1536]{0:T(1024)S(1)} %get-tuple-element.120) | copy-start | bytes 18436
  32.4 351.8 %copy-start.54 = (f32[1536]{0:T(1024)}, f32[1536]{0:T(1024)S(1)}, u32[]{:S(2)}) copy-start(f32[1536]{0:T(1024)S(1)} %get-tuple-element.121) | copy-start | bytes 18436
  32.4 351.8 %copy-start.56 = (f32[1536]{0:T(1024)}, f32[1536]{0:T(1024)S(1)}, u32[]{:S(2)}) copy-start(f32[1536]{0:T(1024)S(1)} %get-tuple-element.122) | copy-start | bytes 18436
  32.4 351.8 %copy-start.58 = (f32[1536]{0:T(1024)}, f32[1536]{0:T(1024)S(1)}, u32[]{:S(2)}) copy-start(f32[1536]{0:T(1024)S(1)} %get-tuple-element.123) | copy-start | bytes 18436
  32.5 351.8 %copy-start.60 = (f32[1536]{0:T(1024)}, f32[1536]{0:T(1024)S(1)}, u32[]{:S(2)}) copy-start(f32[1536]{0:T(1024)S(1)} %get-tuple-element.124) | copy-start | bytes 18436
  32.5 351.8 %copy-start.62 = (f32[1536]{0:T(1024)}, f32[1536]{0:T(1024)S(1)}, u32[]{:S(2)}) copy-start(f32[1536]{0:T(1024)S(1)} %get-tuple-element.125) | copy-start | bytes 18436
  32.5 351.8 %copy-start.64 = (f32[1536]{0:T(1024)}, f32[1536]{0:T(1024)S(1)}, u32[]{:S(2)}) copy-start(f32[1536]{0:T(1024)S(1)} %get-tuple-element.126) | copy-start | bytes 18436
  32.5 351.8 %copy-start.66 = (f32[1536]{0:T(1024)}, f32[1536]{0:T(1024)S(1)}, u32[]{:S(2)}) copy-start(f32[1536]{0:T(1024)S(1)} %get-tuple-element.127) | copy-start | bytes 18436
  32.5 351.8 %copy-start.68 = (f32[1536]{0:T(1024)}, f32[1536]{0:T(1024)S(1)}, u32[]{:S(2)}) copy-start(f32[1536]{0:T(1024)S(1)} %get-tuple-element.128) | copy-start | bytes 18436
  32.5 351.8 %copy-start.70 = (f32[1536]{0:T(1024)}, f32[1536]{0:T(1024)S(1)}, u32[]{:S(2)}) copy-start(f32[1536]{0:T(1024)S(1)} %get-tuple-element.129) | copy-start | bytes 18436
  32.8 351.5 %copy-start.10 = (f32[1536]{0:T(1024)}, f32[1536]{0:T(1024)S(1)}, u32[]{:S(2)}) copy-start(f32[1536]{0:T(1024)S(1)} %get-tuple-element.99) | copy-start | bytes 18436
  32.9 351.5 %copy-start.12 = (f32[1536]{0:T(1024)}, f32[1536]{0:T(1024)S(1)}, u32[]{:S(2)}) copy-start(f32[1536]{0:T(1024)S(1)} %get-tuple-element.100) | copy-start | bytes 18436
  32.9 351.5 %copy-start.14 = (f32[1536]{0:T(1024)}, f32[1536]{0:T(1024)S(1)}, u32[]{:S(2)}) copy-start(f32[1536]{0:T(1024)S(1)} %get-tuple-element.101) | copy-start | bytes 18436
  32.9 351.5 %copy-start.16 = (f32[1536]{0:T(1024)}, f32[1536]{0:T(1024)S(1)}, u32[]{:S(2)}) copy-start(f32[1536]{0:T(1024)S(1)} %get-tuple-element.102) | copy-start | bytes 18436
  32.9 351.5 %copy-start.18 = (f32[1536]{0:T(1024)}, f32[1536]{0:T(1024)S(1)}, u32[]{:S(2)}) copy-start(f32[1536]{0:T(1024)S(1)} %get-tuple-element.103) | copy-start | bytes 18436
  32.9 351.5 %copy-start.20 = (f32[1536]{0:T(1024)}, f32[1536]{0:T(1024)S(1)}, u32[]{:S(2)}) copy-start(f32[1536]{0:T(1024)S(1)} %get-tuple-element.104) | copy-start | bytes 18436
  32.9 351.5 %copy-start.22 = (f32[1536]{0:T(1024)}, f32[1536]{0:T(1024)S(1)}, u32[]{:S(2)}) copy-start(f32[1536]{0:T(1024)S(1)} %get-tuple-element.105) | copy-start | bytes 18436
  32.9 351.5 %copy-start.24 = (f32[1536]{0:T(1024)}, f32[1536]{0:T(1024)S(1)}, u32[]{:S(2)}) copy-start(f32[1536]{0:T(1024)S(1)} %get-tuple-element.106) | copy-start | bytes 18436
  32.9 351.5 %copy-start.26 = (f32[1536]{0:T(1024)}, f32[1536]{0:T(1024)S(1)}, u32[]{:S(2)}) copy-start(f32[1536]{0:T(1024)S(1)} %get-tuple-element.107) | copy-start | bytes 18436
  32.9 351.5 %copy-start.28 = (f32[1536]{0:T(1024)}, f32[1536]{0:T(1024)S(1)}, u32[]{:S(2)}) copy-start(f32[1536]{0:T(1024)S(1)} %get-tuple-element.108) | copy-start | bytes 18436
  32.9 351.5 %copy-start.30 = (f32[1536]{0:T(1024)}, f32[1536]{0:T(1024)S(1)}, u32[]{:S(2)}) copy-start(f32[1536]{0:T(1024)S(1)} %get-tuple-element.109) | copy-start | bytes 18436
  33.0 351.5 %copy-start.32 = (f32[1536]{0:T(1024)}, f32[1536]{0:T(1024)S(1)}, u32[]{:S(2)}) copy-start(f32[1536]{0:T(1024)S(1)} %get-tuple-element.110) | copy-start | bytes 18436
  33.0 351.5 %copy-start.34 = (f32[1536]{0:T(1024)}, f32[1536]{0:T(1024)S(1)}, u32[]{:S(2)}) copy-start(f32[1536]{0:T(1024)S(1)} %get-tuple-element.111) | copy-start | bytes 18436
  586.9 244.2 %collective-permute-start.1 = (bf16[2,15,1536]{2,1,0:T(8,128)(2,1)S(1)}, bf16[2,15,1536]{2,1,0:T(8,128)(2,1)S(1)}, u32[]{:S(2)}, u32[]{:S(2)}) collective-permute-start(bf16[2,15,1536]{2,1,0:T(8,128)(2,1)S(1)} %get-tuple-element.151), channel_id=1, source_target_pairs={{1,0},{2,1},{3,2},{4,3},{5,4},{6,5},{7,6},{8,7},{9,8},{10,9},{11,1... | collective-permute-start | bytes 276488 | tf_op jit(solution)/shard_map/ppermute | solution.py:26
  588.2 244.4 %collective-permute-start = (bf16[2,15,1536]{2,1,0:T(8,128)(2,1)S(1)}, bf16[2,15,1536]{2,1,0:T(8,128)(2,1)S(1)}, u32[]{:S(2)}, u32[]{:S(2)}) collective-permute-start(bf16[2,15,1536]{2,1,0:T(8,128)(2,1)S(1)} %get-tuple-element.150), channel_id=1, source_target_pairs={{0,1},{1,2},{2,3},{3,4},{4,5},{5,6},{6,7},{7,8},{8,9},{9,10},{10,1... | collective-permute-start | bytes 276488 | tf_op jit(solution)/shard_map/ppermute | solution.py:25
  (58 other events, 14621.9 us)
Sparse Core Ops, SparseCore 0:
  30.4 342.0 all-gather.1
  587.0 242.4 all-reduce.1
